TPU v7x, 512 devices: a whole 4x8x8 slice. The times are simulated.
512 devices in a mesh: sec: 2 (over core), atoms: 32 (over z_lo, y), batch: 8 (over z_hi, x).
Axes of the slice: x: 4, y: 8, z: 8 (z_hi: 2, z_lo: 4; z = z_hi * 4 + z_lo), core: 2. Of those that a mesh axis runs over, the one named last changes fastest.
Arguments:
- atoms_in: bfloat16 [8, 16384, 1024], P('batch', 'atoms', 'sec'), may hold values from -6 to 6
- tile_ids: int32 [8, 2, 512], P('batch', None, 'atoms'), may hold values from -1 to 127, as said below
- tile_vals: bfloat16 [8, 512, 128, 128], P('batch', 'atoms'), may hold values from -0.26367188 to 0.26367188
- seq_lens: int32 [8], P('batch'), may hold values from 8193 to 16384, as said below
- pair_labels: int32 [8, 16384], P('batch', 'atoms'), may hold values from 0 to 255
- peak_embed: bfloat16 [8, 256, 256], P('batch', 'sec'), may hold values from -6 to 6
- norm_gain: bfloat16 [1024], P('sec'), may hold values from 0.099609375 to 1.8984375
- w_query: bfloat16 [1024, 512], P(None, 'sec'), may hold values from -0.1875 to 0.1875
- w_key: bfloat16 [1024, 512], P(None, 'sec'), may hold values from -0.1875 to 0.1875
- w_value: bfloat16 [1024, 512], P(None, 'sec'), may hold values from -0.1875 to 0.1875
- w_out: bfloat16 [512, 1024], P('sec'), may hold values from -0.25 to 0.25
- w_proj: bfloat16 [1024, 256], P('sec'), may hold values from -0.1875 to 0.1875
Outputs:
- hidden_two: bfloat16 [8, 16384, 1024], P('batch', 'atoms', 'sec')
- seq_loss: float32 [8], P('batch')
- proj_grad: float32 [8, 1024, 256], P('batch', 'sec')
Inputs may be any that keep to these rules, and one draw needn't show every extreme that they name: `tile_ids`: each index of atoms owns 16 consecutive slots and the row blocks 4 i to 4 (i + 1) - 1; its first 4 slots hold the diagonal tiles of its row blocks; live slots come first and padded slots have both ids -1; every live tile's row block is one of its owner's and its column block lies within 2 blocks of it; in every sequence some index of atoms has all 16 slots live. `seq_lens`: at least one sequence has all 16384 atoms live.
All inputs are finite; a program needn't handle non-finite values.
Results may differ from a plain program's by a relative error of at most 0.013.
Values may be sent and summed in bfloat16 or wider, within the bound.
No kernel may reach another device: no remote copies, remote signals or barrier semaphores. Data moves between devices by JAX's collectives and lax.ppermute only.
A program may use at most 64 MiB of HBM per device.

v0:
```python
import math
import jax
import jax.numpy as jnp
from jax import lax
from jax.sharding import PartitionSpec as P

D = 1024
HEADS = 8
HEAD_DIM = 64
PEAKS = 256
EPSILON = 1e-06
HIGHEST = lax.Precision.HIGHEST


def extended(x, sides, width):
    for axis, dim in sides:
        peers, length = (lax.axis_size(axis), x.shape[dim])
        up = [(i, (i + 1) % peers) for i in range(peers - 1)]
        down = [(j, i) for i, j in up]
        last = lax.slice_in_dim(x, length - width, length, axis=dim)
        leading = lax.slice_in_dim(x, 0, width, axis=dim)
        before = lax.ppermute(last, axis, up)
        after = lax.ppermute(leading, axis, down)
        x = jnp.concatenate([before, x, after], axis=dim)
    return x


def feature_map(values):
    return jax.nn.elu(values) + 1.0


def message_pass(atom_rows, tile_pair, tile_block):
    tile_size = tile_block.shape[-1]
    local_rows, half_width = atom_rows.shape
    block_count = local_rows // tile_size
    reach_blocks = max(block_count // 2, 1)
    padded = extended(atom_rows, (("atoms", 0),), reach_blocks * tile_size)
    blocks = padded.reshape(block_count + 2 * reach_blocks, tile_size, half_width)
    first_block = lax.axis_index("atoms") * block_count
    row_ids = tile_pair[0]
    col_ids = tile_pair[1]
    live_tiles = row_ids >= 0
    col_local = jnp.where(live_tiles, col_ids - first_block + reach_blocks, 0)
    row_local = jnp.where(live_tiles, row_ids - first_block, -1)
    panels = jnp.take(blocks, col_local, axis=0)
    products = jnp.einsum("tij,tjf->tif", tile_block, panels, preferred_element_type=jnp.float32)
    selector = (row_local[None, :] == jnp.arange(block_count, dtype=jnp.int32)[:, None]).astype(
        jnp.float32
    )
    summed = jnp.einsum("bt,tif->bif", selector, products, precision=HIGHEST)
    return summed.reshape(local_rows, half_width).astype(jnp.bfloat16)


def key_summary(key_rows, value_rows, atom_mask, head_count):
    count_rows = key_rows.shape[0]
    feat_keys = (
        feature_map(key_rows.astype(jnp.float32)).reshape(count_rows, head_count, -1)
        * atom_mask[:, None, None]
    )
    value_f = value_rows.astype(jnp.float32).reshape(count_rows, head_count, -1)
    outer_state = jnp.einsum("nhd,nhe->hde", feat_keys, value_f, precision=HIGHEST)
    return (outer_state, jnp.sum(feat_keys, axis=0))


def read_summary(query_rows, outer_state, key_total, head_count):
    count_rows = query_rows.shape[0]
    feat_query = feature_map(query_rows.astype(jnp.float32)).reshape(count_rows, head_count, -1)
    numerator = jnp.einsum("nhd,hde->nhe", feat_query, outer_state, precision=HIGHEST)
    denominator = jnp.einsum("nhd,hd->nh", feat_query, key_total, precision=HIGHEST)
    return (numerator / denominator[..., None]).reshape(count_rows, -1)


def contrast(unit_rows, peak_rows, label_part, mask_part, peak_start):
    logit_scale = 2.0 / math.sqrt(unit_rows.shape[-1])
    peak_f = peak_rows.astype(jnp.float32)
    logits = logit_scale * jnp.dot(unit_rows, peak_f.T, precision=HIGHEST)
    peak_index = peak_start + jnp.arange(peak_rows.shape[0], dtype=jnp.int32)
    target = (label_part[:, None] == peak_index[None, :]).astype(jnp.float32)
    sign_rows = 2.0 * target - 1.0
    loss_part = jnp.sum(mask_part[:, None] * jax.nn.softplus(-sign_rows * logits)) / PEAKS
    slopes = mask_part[:, None] * (jax.nn.sigmoid(logits) - target) * (1.0 / math.sqrt(PEAKS))
    unit_grad = logit_scale * jnp.dot(slopes, peak_f, precision=HIGHEST)
    return (loss_part, unit_grad)


def embed_backward(unit_rows, unit_grad, embed_scale):
    inner_mean = jnp.mean(unit_grad * unit_rows, axis=-1, keepdims=True)
    return (embed_scale * (unit_grad - unit_rows * inner_mean)).astype(jnp.bfloat16)


def shards(
    atoms_in,
    tile_ids,
    tile_vals,
    seq_lens,
    pair_labels,
    peak_embed,
    norm_gain,
    w_query,
    w_key,
    w_value,
    w_out,
    w_proj,
):
    atom_rows = atoms_in[0]
    local_rows = atom_rows.shape[0]
    gathered = message_pass(atom_rows, tile_ids[0], tile_vals[0])
    hidden_one = (atom_rows.astype(jnp.float32) + gathered.astype(jnp.float32)).astype(jnp.bfloat16)
    atom_base = lax.axis_index("atoms") * local_rows
    length_one = seq_lens[0]
    label_row = pair_labels[0]
    peak_part = peak_embed[0]
    hidden_f = hidden_one.astype(jnp.float32)
    square_sum = lax.psum(jnp.sum(hidden_f * hidden_f, axis=-1), "sec")
    row_scale = lax.rsqrt(square_sum[:, None] / D + EPSILON)
    normed = (hidden_f * row_scale * norm_gain.astype(jnp.float32)).astype(jnp.bfloat16)
    head_cols = w_query.shape[1]
    piece_rows = lax.all_gather(normed, "sec", axis=1, tiled=True)
    query_f, key_f, value_f = tuple(
        (
            jnp.dot(piece_rows, weight, preferred_element_type=jnp.float32)
            for weight in (w_query, w_key, w_value)
        )
    )
    head_count = head_cols // HEAD_DIM
    atom_mask = (atom_base + jnp.arange(local_rows, dtype=jnp.int32) < length_one).astype(
        jnp.float32
    )
    outer_state, key_total = key_summary(
        key_f.astype(jnp.bfloat16), value_f.astype(jnp.bfloat16), atom_mask, head_count
    )
    outer_state, key_total = lax.psum((outer_state, key_total), "atoms")
    attended = read_summary(query_f.astype(jnp.bfloat16), outer_state, key_total, head_count)
    out_sum = lax.psum(jnp.sum(attended * attended, axis=-1), "sec")
    attended_n = (attended * lax.rsqrt(out_sum[:, None] / (HEADS * HEAD_DIM) + EPSILON)).astype(
        jnp.bfloat16
    )
    branch_full = jnp.dot(attended_n, w_out, preferred_element_type=jnp.float32)
    branch = lax.psum_scatter(branch_full, "sec", scatter_dimension=1, tiled=True)
    hidden_two = (hidden_f + branch).astype(jnp.bfloat16)
    embedded = lax.psum(jnp.dot(hidden_two, w_proj, preferred_element_type=jnp.float32), "sec")
    embed_scale = lax.rsqrt(jnp.mean(embedded * embedded, axis=-1, keepdims=True) + EPSILON)
    unit_rows = embedded * embed_scale
    peak_start = lax.axis_index("sec") * peak_part.shape[0]
    loss_part, unit_grad = contrast(unit_rows, peak_part, label_row, atom_mask, peak_start)
    unit_grad = lax.psum(unit_grad, "sec")
    embed_grad = embed_backward(unit_rows, unit_grad, embed_scale)
    proj_part = jnp.einsum("nd,ne->de", hidden_two, embed_grad, preferred_element_type=jnp.float32)
    loss_total = lax.psum(loss_part, ("sec", "atoms")) / (local_rows * lax.axis_size("atoms"))
    proj_total = lax.psum(proj_part, "atoms")
    return (hidden_two[None], loss_total.reshape(1), proj_total[None])


def solution(mesh):
    return jax.shard_map(
        shards,
        mesh=mesh,
        in_specs=(
            P("batch", "atoms", "sec"),
            P("batch", None, "atoms"),
            P("batch", "atoms", None, None),
            P("batch"),
            P("batch", "atoms"),
            P("batch", "sec", None),
            P("sec"),
            P(None, "sec"),
            P(None, "sec"),
            P(None, "sec"),
            P("sec", None),
            P("sec", None),
        ),
        out_specs=(P("batch", "atoms", "sec"), P("batch"), P("batch", "sec", None)),
        check_vma=False,
    )
```

profile of v0, /device:TPU:2, one launch (start us, length us, event | category | flops | bytes accessed | tf_op | source)
XLA Modules:
  0.0 773.8 jit_solution(17922998423100423061)
XLA Ops:
  7.2 1.1 slice_bitcast_fusion.1
  8.3 3.5 collective-permute-start
  11.8 1.3 collective-permute-start.1
  13.2 0.8 compare_and_fusion
  13.9 0.7 convert_element_type.72
  14.6 0.7 fusion.57
  15.3 2.1 collective-permute-done
  17.4 4.1 collective-permute-done.1
  21.5 1.1 pad_maximum_fusion
  22.6 2.0 gather_fusion
  24.6 4.4 fusion.2
  29.0 5.5 copy.16
  34.5 3.7 fusion.8
  38.3 0.3 copy.15
  38.6 0.7 copy-done.1
  39.3 0.2 fusion.14
  39.5 2.6 psum.56
  42.1 1.0 fusion.16
  43.2 0.0 all-reduce.5.cloned.1.call-start
  43.9 21.4 %all-gather.2.cloned.1.call-done = bf16[512,1024]{1,0:T(8,128)(2,1)} async-done(((bf16[512,512]{1,0:T(8,128)(2,1)}), bf16[512,1024]{1,0:T(8,128)(2,1)}) %all-gather.2.cloned.1.call-update) | async-done | bytes 1048592 | tf_op jit(solution)/shard_map/all_gather | solution.py:118
  65.3 1.7 convolution_convert_fusion.1
  67.0 2.1 multiply_reduce_fusion.3
  69.1 1.1 fusion.26
  70.2 0.0 reduce-scatter.2.cloned.1.call-start
  70.3 0.1 reduce_sum.58
  70.4 80.4 %psum.58 = f32[4,64]{1,0:T(4,128)S(1)} all-reduce(f32[4,64]{1,0:T(4,128)S(1)} %reduce_sum.58), channel_id=1, replica_groups=mesh['sec'=2,'atoms'=32,'batch'=8] {'atoms'}, use_global_device_ids=true, to_apply=%region_4.5 | all-reduce | flops 256 | bytes 2048 | tf_op jit(solution)/shard_map/psum | solution.py:132
  150.8 1.7 fusion.23
  152.5 0.4 fusion.63
  152.8 197.0 %all-reduce.5.cloned.1.call-done = f32[4,64,64]{1,2,0:T(8,128)} async-done(((f32[4,64,64]{1,2,0:T(8,128)}), f32[4,64,64]{1,2,0:T(8,128)}) %all-reduce.5.cloned.1.call-update) | async-done | bytes 65552 | tf_op jit(solution)/shard_map/psum | solution.py:132
  349.8 1.5 multiply_reduce_fusion.2
  351.3 2.5 psum.59
  353.8 1.8 fusion.64
  355.7 0.0 all-reduce.7.cloned.1.call-start
  355.8 14.7 %reduce-scatter.2.cloned.1.call-done = f32[512,512]{1,0:T(8,128)} async-done(((f32[512,1024]{1,0:T(8,128)}), f32[512,512]{1,0:T(8,128)}) %reduce-scatter.2.cloned.1.call-update) | async-done | bytes 1048592 | tf_op jit(solution)/shard_map/reduce_scatter | solution.py:139
  370.5 1.4 fusion.17
  371.9 1.1 fusion.65
  373.0 0.0 all-reduce.9.cloned.1.call-start
  373.1 37.2 %all-reduce.7.cloned.1.call-done = f32[512,256]{1,0:T(8,128)} async-done(((f32[512,256]{1,0:T(8,128)}), f32[512,256]{1,0:T(8,128)}) %all-reduce.7.cloned.1.call-update) | async-done | bytes 524304 | tf_op jit(solution)/shard_map/psum | solution.py:141
  410.3 1.3 multiply_reduce_fusion.1
  411.6 2.2 fusion.37
  413.8 1.3 convolution_multiply_fusion
  415.1 0.0 all-reduce.11.cloned.1.call-start
  415.1 36.6 %all-reduce.9.cloned.1.call-done = f32[512,256]{1,0:T(8,128)} async-done(((f32[512,256]{1,0:T(8,128)}), f32[512,256]{1,0:T(8,128)}) %all-reduce.9.cloned.1.call-update) | async-done | bytes 524304 | tf_op jit(solution)/shard_map/psum | solution.py:146
  451.7 1.3 multiply_reduce_fusion
  453.0 2.3 convolution_bitcast_fusion
  456.0 141.1 %psum.61 = f32[]{:T(128)} all-reduce(f32[]{:T(128)S(6)} %div.42), channel_id=1, replica_groups=mesh['sec'=2,'atoms'=32,'batch'=8] {'sec','atoms'}, use_global_device_ids=true, to_apply=%region_11.12 | all-reduce | flops 1 | bytes 8 | tf_op jit(solution)/shard_map/psum | solution.py:149
  597.7 166.3 %all-reduce.11.cloned.1.call-done = f32[1,512,256]{2,1,0:T(8,128)} async-done(((f32[1,512,256]{2,1,0:T(8,128)}), f32[1,512,256]{2,1,0:T(8,128)}) %all-reduce.11.cloned.1.call-update) | async-done | bytes 524304 | tf_op jit(solution)/shard_map/psum | solution.py:150
  764.0 1.9 copy.26
  (38 shorter events, 0.3 us)
Async XLA Ops:
  7.2 17.5 %copy-start = (bf16[1,16,128,128]{3,2,1,0:T(8,128)(2,1)S(1)}, bf16[1,16,128,128]{3,2,1,0:T(8,128)(2,1)}, u32[]{:S(2)}) copy-start(bf16[1,16,128,128]{3,2,1,0:T(8,128)(2,1)} %param.14) | copy-start | bytes 1572868
  7.2 58.1 %all-gather.2.cloned.1.call-start = ((), (), s32[]{:S(2)}) async-start(), calls=%async_computation.1 | async-start | bytes 1572864 | tf_op jit(solution)/shard_map/all_gather | solution.py:118
  8.3 9.0 %collective-permute-start = (bf16[256,512]{1,0:T(8,128)(2,1)S(1)}, bf16[256,512]{1,0:T(8,128)(2,1)S(1)}, u32[]{:S(2)}, u32[]{:S(2)}) collective-permute-start(bf16[256,512]{1,0:T(8,128)(2,1)S(1)} %get-tuple-element.7), channel_id=1, source_target_pairs={{0,8},{8,16},{16,24},{24,32},{32,40},{40,48},{48,56},{56,64},{64,7... | collective-permute-start | bytes 786440 | tf_op jit(solution)/shard_map/ppermute | solution.py:22
  11.8 9.7 %collective-permute-start.1 = (bf16[256,512]{1,0:T(8,128)(2,1)S(1)}, bf16[256,512]{1,0:T(8,128)(2,1)S(1)}, u32[]{:S(2)}, u32[]{:S(2)}) collective-permute-start(bf16[256,512]{1,0:T(8,128)(2,1)S(1)} %get-tuple-element.8), channel_id=1, source_target_pairs={{8,0},{16,8},{24,16},{32,24},{40,32},{48,40},{56,48},{64,56},{72,6... | collective-permute-start | bytes 786440 | tf_op jit(solution)/shard_map/ppermute | solution.py:23
  38.3 1.0 copy-start.1
  39.3 26.0 %copy-start.5 = (bf16[1024,256]{1,0:T(8,128)(2,1)S(1)}, bf16[1024,256]{1,0:T(8,128)(2,1)}, u32[]{:S(2)}) copy-start(bf16[1024,256]{1,0:T(8,128)(2,1)} %param.21) | copy-start | bytes 1572868
  39.5 27.5 %copy-start.8 = (bf16[1024,256]{1,0:T(8,128)(2,1)S(1)}, bf16[1024,256]{1,0:T(8,128)(2,1)}, u32[]{:S(2)}) copy-start(bf16[1024,256]{1,0:T(8,128)(2,1)} %param.20) | copy-start | bytes 1572868
  43.2 306.6 %all-reduce.5.cloned.1.call-start = ((), (), s32[]{:S(2)}) async-start(), calls=%async_computation.2 | async-start | bytes 262144 | tf_op jit(solution)/shard_map/psum | solution.py:132
  67.0 83.7 %copy-start.4 = (bf16[512,1024]{1,0:T(8,128)(2,1)S(1)}, bf16[512,1024]{1,0:T(8,128)(2,1)}, u32[]{:S(2)}) copy-start(bf16[512,1024]{1,0:T(8,128)(2,1)} %all-gather.2.cloned.1.call-done) | copy-start | bytes 3145732
  70.2 300.3 %reduce-scatter.2.cloned.1.call-start = ((), (), s32[]{:S(2)}) async-start(), calls=%async_computation.3 | async-start | bytes 3145728 | tf_op jit(solution)/shard_map/reduce_scatter | solution.py:139
  152.4 201.4 %copy-start.6 = (bf16[256,1024]{1,0:T(8,128)(2,1)S(1)}, bf16[256,1024]{1,0:T(8,128)(2,1)}, u32[]{:S(2)}) copy-start(bf16[256,1024]{1,0:T(8,128)(2,1)} %param.22) | copy-start | bytes 1572868
  355.7 16.2 %copy-start.7 = (bf16[512,256]{1,0:T(8,128)(2,1)S(1)}, bf16[512,256]{1,0:T(8,128)(2,1)}, u32[]{:S(2)}) copy-start(bf16[512,256]{1,0:T(8,128)(2,1)} %param.23) | copy-start | bytes 786436
  355.7 55.9 %copy-start.9 = (bf16[1,128,256]{2,1,0:T(8,128)(2,1)S(1)}, bf16[1,128,256]{2,1,0:T(8,128)(2,1)}, u32[]{:S(2)}) copy-start(bf16[1,128,256]{2,1,0:T(8,128)(2,1)} %param.17) | copy-start | bytes 196612
  355.7 55.9 %copy-start.10 = (s32[1,512]{1,0:T(1,128)S(1)}, s32[1,512]{1,0:T(1,128)}, u32[]{:S(2)}) copy-start(s32[1,512]{1,0:T(1,128)} %param.16) | copy-start | bytes 6148
  355.7 54.6 %all-reduce.7.cloned.1.call-start = ((), (), s32[]{:S(2)}) async-start(), calls=%async_computation.4 | async-start | bytes 1048576 | tf_op jit(solution)/shard_map/psum | solution.py:141
  371.9 81.1 %copy-start.3 = (bf16[512,512]{1,0:T(8,128)(2,1)}, bf16[512,512]{1,0:T(8,128)(2,1)S(1)}, u32[]{:S(2)}) copy-start(bf16[512,512]{1,0:T(8,128)(2,1)S(1)} %fusion.17) | copy-start | bytes 1572868
  373.0 78.6 %all-reduce.9.cloned.1.call-start = ((), (), s32[]{:S(2)}) async-start(), calls=%async_computation.5 | async-start | bytes 1048576 | tf_op jit(solution)/shard_map/psum | solution.py:146
  410.3 41.4 %copy-start.2 = (f32[512,256]{1,0:T(8,128)S(1)}, f32[512,256]{1,0:T(8,128)}, u32[]{:S(2)}) copy-start(f32[512,256]{1,0:T(8,128)} %all-reduce.7.cloned.1.call-done) | copy-start | bytes 1572868
  415.1 348.9 %all-reduce.11.cloned.1.call-start = ((), (), s32[]{:S(2)}) async-start(), calls=%async_computation.6 | async-start | bytes 1048576 | tf_op jit(solution)/shard_map/psum | solution.py:150
Sparse Core Ops, SparseCore 0:
  43.3 21.9 all-gather.1
  70.4 279.3 all-reduce.4
  355.8 14.6 reduce-scatter.1
  373.8 36.4 all-reduce.6
  415.2 36.4 all-reduce.8
  455.4 308.4 all-reduce.10
where the time goes:
time: 775 us; the launch traced here: 774 us
  waiting for transfers between devices  479 us (62%)
  blocking collectives  227 us (29%)
  matrix products  25.2 us (3%)
  between operations  17.4 us (2%)
  local copies, waits for them, and re-layouts  11.7 us (2%)
  other arithmetic  8.46 us (1%)
    psum x1, waiting for transfers between devices, shards(): outer_state, key_total = lax.psum((outer_state, key_total), 'atoms')  197 us
    psum x1, waiting for transfers between devices, shards(): proj_total = lax.psum(proj_part, 'atoms')  166 us
    psum x1, blocking collectives, shards(): lax.psum(loss_part, ('sec', 'atoms'))  141 us
    psum x1, blocking collectives, shards(): outer_state, key_total = lax.psum((outer_state, key_total), 'atoms')  80.4 us
    psum x1, waiting for transfers between devices, shards(): lax.psum(jnp.dot(hidden_two, w_proj, preferred_element_type=jnp.float32),...  37.2 us
    psum x1, waiting for transfers between devices, shards(): unit_grad = lax.psum(unit_grad, 'sec')  36.6 us
    all_gather x1, waiting for transfers between devices, shards(): piece_rows = lax.all_gather(normed, 'sec', axis=1, tiled=True)  21.4 us
  transfers between devices with their start and end apart: 8, of which 8 were waited for; matrix products, arithmetic and copies ran while one was open for 1% of the time, Pallas kernels for 0%

commit v1 on v0

--- a/solution.py
+++ b/solution.py
@@ -138,7 +138,8 @@
     branch_full = jnp.dot(attended_n, w_out, preferred_element_type=jnp.float32)
     branch = lax.psum_scatter(branch_full, "sec", scatter_dimension=1, tiled=True)
     hidden_two = (hidden_f + branch).astype(jnp.bfloat16)
-    embedded = lax.psum(jnp.dot(hidden_two, w_proj, preferred_element_type=jnp.float32), "sec")
+    frame = jnp.dot(hidden_two, w_proj, preferred_element_type=jnp.float32)
+    embedded = lax.all_gather(frame, "sec").sum(axis=0)
     embed_scale = lax.rsqrt(jnp.mean(embedded * embedded, axis=-1, keepdims=True) + EPSILON)
     unit_rows = embedded * embed_scale
     peak_start = lax.axis_index("sec") * peak_part.shape[0]

time: 775 us -> 755 us (0.974)
  waiting for transfers between devices: 479 us -> 461 us
    psum x1 -> x0, waiting for transfers between devices: 37.2 us -> none  [shards(): lax.psum(jnp.dot(hidden_two, w_proj, preferred_element_type=jnp.float32),...]
    all_gather x0 -> x1, waiting for transfers between devices: none -> 18.6 us  [shards(): embedded = lax.all_gather(frame, 'sec').sum(axis=0)]
where the time goes in v1:
time: 755 us; the launch traced here: 754 us
  waiting for transfers between devices  461 us (61%)
  blocking collectives  227 us (30%)
  matrix products  24.2 us (3%)
  between operations  17.4 us (2%)
  local copies, waits for them, and re-layouts  11.7 us (2%)
  other arithmetic  8.7 us (1%)
    psum x1, waiting for transfers between devices, shards(): outer_state, key_total = lax.psum((outer_state, key_total), 'atoms')  197 us
    psum x1, waiting for transfers between devices, shards(): proj_total = lax.psum(proj_part, 'atoms')  166 us
    psum x1, blocking collectives, shards(): lax.psum(loss_part, ('sec', 'atoms'))  141 us
    psum x1, blocking collectives, shards(): outer_state, key_total = lax.psum((outer_state, key_total), 'atoms')  80.4 us
    psum x1, waiting for transfers between devices, shards(): unit_grad = lax.psum(unit_grad, 'sec')  36.6 us
    all_gather x1, waiting for transfers between devices, shards(): piece_rows = lax.all_gather(normed, 'sec', axis=1, tiled=True)  21.4 us
    all_gather x1, waiting for transfers between devices, shards(): embedded = lax.all_gather(frame, 'sec').sum(axis=0)  18.6 us
  transfers between devices with their start and end apart: 8, of which 8 were waited for; matrix products, arithmetic and copies ran while one was open for 1% of the time, Pallas kernels for 0%

profile of v1, /device:TPU:2, one launch (start us, length us, event | category | flops | bytes accessed | tf_op | source)
XLA Modules:
  0.0 754.4 jit_solution(17879233798281418117)
XLA Ops:
  7.2 1.1 slice_bitcast_fusion.1
  8.3 3.5 collective-permute-start
  11.8 1.3 collective-permute-start.1
  13.2 0.8 compare_and_fusion
  13.9 0.7 convert_element_type.72
  14.6 0.7 fusion.57
  15.3 2.1 collective-permute-done
  17.4 4.1 collective-permute-done.1
  21.5 1.1 pad_maximum_fusion
  22.6 2.0 gather_fusion
  24.6 4.4 fusion.2
  29.0 5.5 copy.16
  34.5 3.7 fusion.8
  38.3 0.3 copy.15
  38.6 0.7 copy-done.1
  39.3 0.2 fusion.14
  39.5 2.6 psum.49
  42.1 1.0 fusion.16
  43.2 0.0 all-reduce.4.cloned.1.call-start
  43.9 21.4 %all-gather.4.cloned.1.call-done = bf16[512,1024]{1,0:T(8,128)(2,1)} async-done(((bf16[512,512]{1,0:T(8,128)(2,1)}), bf16[512,1024]{1,0:T(8,128)(2,1)}) %all-gather.4.cloned.1.call-update) | async-done | bytes 1048592 | tf_op jit(solution)/shard_map/all_gather | solution.py:118
  65.3 1.7 convolution_convert_fusion.1
  67.0 2.1 multiply_reduce_fusion.3
  69.1 1.1 fusion.26
  70.2 0.0 reduce-scatter.2.cloned.1.call-start
  70.3 0.1 reduce_sum.67
  70.4 80.4 %psum.51 = f32[4,64]{1,0:T(4,128)S(1)} all-reduce(f32[4,64]{1,0:T(4,128)S(1)} %reduce_sum.67), channel_id=1, replica_groups=mesh['sec'=2,'atoms'=32,'batch'=8] {'atoms'}, use_global_device_ids=true, to_apply=%region_4.5 | all-reduce | flops 256 | bytes 2048 | tf_op jit(solution)/shard_map/psum | solution.py:132
  150.8 1.7 fusion.23
  152.5 0.4 fusion.63
  152.8 197.0 %all-reduce.4.cloned.1.call-done = f32[4,64,64]{1,2,0:T(8,128)} async-done(((f32[4,64,64]{1,2,0:T(8,128)}), f32[4,64,64]{1,2,0:T(8,128)}) %all-reduce.4.cloned.1.call-update) | async-done | bytes 65552 | tf_op jit(solution)/shard_map/psum | solution.py:132
  349.8 1.5 multiply_reduce_fusion.2
  351.3 2.5 psum.52
  353.8 1.8 fusion.64
  355.8 14.8 %reduce-scatter.2.cloned.1.call-done = f32[512,512]{1,0:T(8,128)} async-done(((f32[512,1024]{1,0:T(8,128)}), f32[512,512]{1,0:T(8,128)}) %reduce-scatter.2.cloned.1.call-update) | async-done | bytes 1048592 | tf_op jit(solution)/shard_map/reduce_scatter | solution.py:139
  370.5 1.4 fusion.17
  371.9 1.1 fusion.65
  373.1 0.0 all-reduce.6.cloned.1.call-start
  373.1 18.6 %all-gather.6.cloned.1.call-done = f32[1024,256]{1,0:T(8,128)} async-done(((f32[512,256]{1,0:T(8,128)}), f32[1024,256]{1,0:T(8,128)}) %all-gather.6.cloned.1.call-update) | async-done | bytes 1048592 | tf_op jit(solution)/shard_map/all_gather | solution.py:142
  391.7 1.4 reduce_sum.69
  393.1 0.1 multiply_reduce_fusion.1
  393.2 1.1 fusion.37
  394.4 1.3 convolution_multiply_fusion
  395.6 0.0 all-reduce.8.cloned.1.call-start
  395.7 36.6 %all-reduce.6.cloned.1.call-done = f32[512,256]{1,0:T(8,128)} async-done(((f32[512,256]{1,0:T(8,128)}), f32[512,256]{1,0:T(8,128)}) %all-reduce.6.cloned.1.call-update) | async-done | bytes 524304 | tf_op jit(solution)/shard_map/psum | solution.py:147
  432.2 1.3 multiply_reduce_fusion
  433.5 2.3 convolution_bitcast_fusion
  436.5 141.1 %psum.53 = f32[]{:T(128)} all-reduce(f32[]{:T(128)S(6)} %div.42), channel_id=1, replica_groups=mesh['sec'=2,'atoms'=32,'batch'=8] {'sec','atoms'}, use_global_device_ids=true, to_apply=%region_11.12 | all-reduce | flops 1 | bytes 8 | tf_op jit(solution)/shard_map/psum | solution.py:150
  578.3 166.3 %all-reduce.8.cloned.1.call-done = f32[1,512,256]{2,1,0:T(8,128)} async-done(((f32[1,512,256]{2,1,0:T(8,128)}), f32[1,512,256]{2,1,0:T(8,128)}) %all-reduce.8.cloned.1.call-update) | async-done | bytes 524304 | tf_op jit(solution)/shard_map/psum | solution.py:151
  744.5 1.9 copy.25
  (37 shorter events, 0.3 us)
Async XLA Ops:
  7.2 17.5 %copy-start = (bf16[1,16,128,128]{3,2,1,0:T(8,128)(2,1)S(1)}, bf16[1,16,128,128]{3,2,1,0:T(8,128)(2,1)}, u32[]{:S(2)}) copy-start(bf16[1,16,128,128]{3,2,1,0:T(8,128)(2,1)} %param.14) | copy-start | bytes 1572868
  7.2 58.1 %all-gather.4.cloned.1.call-start = ((), (), s32[]{:S(2)}) async-start(), calls=%async_computation.1 | async-start | bytes 1572864 | tf_op jit(solution)/shard_map/all_gather | solution.py:118
  8.3 9.0 %collective-permute-start = (bf16[256,512]{1,0:T(8,128)(2,1)S(1)}, bf16[256,512]{1,0:T(8,128)(2,1)S(1)}, u32[]{:S(2)}, u32[]{:S(2)}) collective-permute-start(bf16[256,512]{1,0:T(8,128)(2,1)S(1)} %get-tuple-element.7), channel_id=1, source_target_pairs={{0,8},{8,16},{16,24},{24,32},{32,40},{40,48},{48,56},{56,64},{64,7... | collective-permute-start | bytes 786440 | tf_op jit(solution)/shard_map/ppermute | solution.py:22
  11.8 9.7 %collective-permute-start.1 = (bf16[256,512]{1,0:T(8,128)(2,1)S(1)}, bf16[256,512]{1,0:T(8,128)(2,1)S(1)}, u32[]{:S(2)}, u32[]{:S(2)}) collective-permute-start(bf16[256,512]{1,0:T(8,128)(2,1)S(1)} %get-tuple-element.8), channel_id=1, source_target_pairs={{8,0},{16,8},{24,16},{32,24},{40,32},{48,40},{56,48},{64,56},{72,6... | collective-permute-start | bytes 786440 | tf_op jit(solution)/shard_map/ppermute | solution.py:23
  38.3 1.0 copy-start.1
  39.3 26.0 %copy-start.4 = (bf16[1024,256]{1,0:T(8,128)(2,1)S(1)}, bf16[1024,256]{1,0:T(8,128)(2,1)}, u32[]{:S(2)}) copy-start(bf16[1024,256]{1,0:T(8,128)(2,1)} %param.21) | copy-start | bytes 1572868
  39.5 27.5 %copy-start.7 = (bf16[1024,256]{1,0:T(8,128)(2,1)S(1)}, bf16[1024,256]{1,0:T(8,128)(2,1)}, u32[]{:S(2)}) copy-start(bf16[1024,256]{1,0:T(8,128)(2,1)} %param.20) | copy-start | bytes 1572868
  43.2 306.6 %all-reduce.4.cloned.1.call-start = ((), (), s32[]{:S(2)}) async-start(), calls=%async_computation.2 | async-start | bytes 262144 | tf_op jit(solution)/shard_map/psum | solution.py:132
  67.0 83.7 %copy-start.3 = (bf16[512,1024]{1,0:T(8,128)(2,1)S(1)}, bf16[512,1024]{1,0:T(8,128)(2,1)}, u32[]{:S(2)}) copy-start(bf16[512,1024]{1,0:T(8,128)(2,1)} %all-gather.4.cloned.1.call-done) | copy-start | bytes 3145732
  70.2 300.3 %reduce-scatter.2.cloned.1.call-start = ((), (), s32[]{:S(2)}) async-start(), calls=%async_computation.3 | async-start | bytes 3145728 | tf_op jit(solution)/shard_map/reduce_scatter | solution.py:139
  152.4 201.4 %copy-start.5 = (bf16[256,1024]{1,0:T(8,128)(2,1)S(1)}, bf16[256,1024]{1,0:T(8,128)(2,1)}, u32[]{:S(2)}) copy-start(bf16[256,1024]{1,0:T(8,128)(2,1)} %param.22) | copy-start | bytes 1572868
  355.7 16.2 %copy-start.6 = (bf16[512,256]{1,0:T(8,128)(2,1)S(1)}, bf16[512,256]{1,0:T(8,128)(2,1)}, u32[]{:S(2)}) copy-start(bf16[512,256]{1,0:T(8,128)(2,1)} %param.23) | copy-start | bytes 786436
  355.7 36.0 %all-gather.6.cloned.1.call-start = ((), (), s32[]{:S(2)}) async-start(), calls=%async_computation.6 | async-start | bytes 1572864 | tf_op jit(solution)/shard_map/all_gather | solution.py:142
  371.9 61.6 %copy-start.2 = (bf16[512,512]{1,0:T(8,128)(2,1)}, bf16[512,512]{1,0:T(8,128)(2,1)S(1)}, u32[]{:S(2)}) copy-start(bf16[512,512]{1,0:T(8,128)(2,1)S(1)} %fusion.17) | copy-start | bytes 1572868
  371.9 21.3 %copy-start.8 = (bf16[1,128,256]{2,1,0:T(8,128)(2,1)S(1)}, bf16[1,128,256]{2,1,0:T(8,128)(2,1)}, u32[]{:S(2)}) copy-start(bf16[1,128,256]{2,1,0:T(8,128)(2,1)} %param.17) | copy-start | bytes 196612
  371.9 21.3 %copy-start.9 = (s32[1,512]{1,0:T(1,128)S(1)}, s32[1,512]{1,0:T(1,128)}, u32[]{:S(2)}) copy-start(s32[1,512]{1,0:T(1,128)} %param.16) | copy-start | bytes 6148
  373.1 59.2 %all-reduce.6.cloned.1.call-start = ((), (), s32[]{:S(2)}) async-start(), calls=%async_computation.4 | async-start | bytes 1048576 | tf_op jit(solution)/shard_map/psum | solution.py:147
  395.6 348.9 %all-reduce.8.cloned.1.call-start = ((), (), s32[]{:S(2)}) async-start(), calls=%async_computation.5 | async-start | bytes 1048576 | tf_op jit(solution)/shard_map/psum | solution.py:151
Sparse Core Ops, SparseCore 0:
  43.3 21.9 all-gather.3
  70.4 279.3 all-reduce.3
  355.8 14.6 reduce-scatter.1
  373.2 18.4 all-gather.5
  395.8 36.4 all-reduce.5
  436.0 308.4 all-reduce.7
